TPU v7x, 512 devices: a whole 4x4x16 slice. The times are simulated.
512 devices in a mesh: pipe: 4 (over y), expert: 32 (over z, core), tensor: 4 (over x).
Axes of the slice: x: 4, y: 4, z: 16, core: 2. Of those that a mesh axis runs over, the one named last changes fastest.
Arguments:
- tokens: bfloat16 [512, 6144], P('expert', ('pipe', 'tensor')), may hold values from -6 to 6
- expert_ids: int32 [512, 2], P('expert'), may hold values from 0 to 7, all different within a row; in each aligned block of 16 rows (0 to 15, 16 to 31, ...) at most 5 rows name the same one
- gates: float32 [512, 2], P('expert'), may hold values from 0.2 to 1
- w_gate: bfloat16 [32, 6144, 2048], P('expert', None, ('pipe', 'tensor')), may hold values from -0.078125 to 0.078125
- w_up: bfloat16 [32, 6144, 2048], P('expert', None, ('pipe', 'tensor')), may hold values from -0.078125 to 0.078125
- w_down: bfloat16 [32, 2048, 6144], P('expert', ('pipe', 'tensor')), may hold values from -0.0625 to 0.0625
- d_out: bfloat16 [512, 6144], P('expert', ('pipe', 'tensor')), may hold values from -6 to 6
Outputs:
- moe_out: bfloat16 [512, 6144], P('expert', ('pipe', 'tensor'))
- grad_tokens: bfloat16 [512, 6144], P('expert', ('pipe', 'tensor'))
- grad_gates: float32 [512, 2], P('expert')
Inputs may be any that keep to these rules, and one draw needn't show every extreme that they name: `expert_ids`: each row names 2 different experts. Among the rows of one index of expert (aligned blocks of 16 rows) no expert is named more than 5 times, a bound that some block reaches.
All inputs are finite; a program needn't handle non-finite values.
Results may differ from a plain program's by a relative error of at most 0.017.
Values may be sent and summed in bfloat16 or wider, within the bound.
No kernel may reach another device: no remote copies, remote signals or barrier semaphores. Data moves between devices by JAX's collectives and lax.ppermute only.
A program may use at most 64 MiB of HBM per device.

v0:
```python
import jax
import jax.numpy as jnp
from jax import lax
from jax.sharding import PartitionSpec as P


def per_device(tokens, expert_ids, gates, w_gate, w_up, w_down, d_out):
    tok_rows = tokens.shape[0]
    feat = tokens.shape[1]
    top = expert_ids.shape[1]
    devices_all = lax.axis_size("expert")
    experts = min(8, devices_all)
    group = devices_all // experts
    capacity = min(
        tok_rows,
        max(2, max(5 * tok_rows * top // (4 * experts), (tok_rows * top + experts - 1) // experts)),
    )
    slots = experts * capacity
    flat_ids = expert_ids.reshape(-1)
    onehot = (flat_ids[:, None] == jnp.arange(experts, dtype=jnp.int32)[None, :]).astype(jnp.int32)
    position = jnp.sum(jnp.cumsum(onehot, axis=0) * onehot, axis=1) - 1
    slot_of = flat_ids * capacity + position
    picks = (jnp.arange(slots, dtype=jnp.int32)[:, None] == slot_of[None, :]).astype(jnp.float32)
    pick_rows = picks.reshape(slots, tok_rows, top)
    select_tok = jnp.sum(pick_rows, axis=2).astype(jnp.bfloat16)
    select_gate = jnp.sum(pick_rows * gates[None, :, :], axis=2)
    picked = jnp.dot(select_tok, tokens, preferred_element_type=jnp.float32).astype(jnp.bfloat16)
    scaled = jnp.dot(
        select_gate, d_out.astype(jnp.float32), precision=lax.Precision.HIGHEST
    ).astype(jnp.bfloat16)
    send = jnp.concatenate([picked, scaled], axis=1).reshape(experts, capacity, 2 * feat)
    send = jnp.repeat(send, group, axis=0)
    recv = lax.all_to_all(send, "expert", split_axis=0, concat_axis=0, tiled=True)
    recv = recv.reshape(devices_all * capacity, 2 * feat)
    part_x = recv[:, :feat]
    part_dy = recv[:, feat:]
    rows_x = lax.all_gather(part_x, ("pipe", "tensor"), axis=1, tiled=True)
    rows_dy = lax.all_gather(part_dy, ("pipe", "tensor"), axis=1, tiled=True)
    gate_proj = w_gate[0]
    up_proj = w_up[0]
    down_proj = w_down[0]
    contract_last = (((1,), (1,)), ((), ()))
    h_gate = jnp.dot(rows_x, gate_proj, preferred_element_type=jnp.float32)
    h_up = jnp.dot(rows_x, up_proj, preferred_element_type=jnp.float32)
    sig = jax.nn.sigmoid(h_gate)
    hidden = (h_gate * sig * h_up).astype(jnp.bfloat16)
    out_terms = jnp.dot(hidden, down_proj, preferred_element_type=jnp.float32)
    d_hidden = lax.dot_general(
        rows_dy, down_proj, contract_last, preferred_element_type=jnp.float32
    )
    d_gate_h = (d_hidden * h_up * sig * (1.0 + h_gate * (1.0 - sig))).astype(jnp.bfloat16)
    d_up_h = (d_hidden * h_gate * sig).astype(jnp.bfloat16)
    dx_terms = lax.dot_general(
        d_gate_h, gate_proj, contract_last, preferred_element_type=jnp.float32
    )
    dx_terms = dx_terms + lax.dot_general(
        d_up_h, up_proj, contract_last, preferred_element_type=jnp.float32
    )
    out_share = lax.psum_scatter(
        out_terms.astype(jnp.bfloat16), ("pipe", "tensor"), scatter_dimension=1, tiled=True
    )
    dx_share = lax.psum_scatter(
        dx_terms.astype(jnp.bfloat16), ("pipe", "tensor"), scatter_dimension=1, tiled=True
    )
    back_send = jnp.concatenate([out_share, dx_share], axis=1).reshape(
        devices_all, capacity, 2 * feat
    )
    back = lax.all_to_all(back_send, "expert", split_axis=0, concat_axis=0, tiled=True)
    back_rows = (
        jnp.sum(back.astype(jnp.float32).reshape(experts, group, capacity, 2 * feat), axis=1)
        .astype(jnp.bfloat16)
        .reshape(slots, 2 * feat)
    )
    assign = picks.T.astype(jnp.bfloat16)
    a_both = jnp.dot(assign, back_rows, preferred_element_type=jnp.float32)
    a_out = a_both[:, :feat].reshape(tok_rows, top, feat)
    a_dx = a_both[:, feat:].reshape(tok_rows, top, feat)
    moe_out = jnp.sum(gates[:, :, None] * a_out, axis=1).astype(jnp.bfloat16)
    grad_tokens = jnp.sum(a_dx, axis=1).astype(jnp.bfloat16)
    partial_dots = jnp.sum(d_out.astype(jnp.float32)[:, None, :] * a_out, axis=2)
    grad_gates = lax.psum(partial_dots, ("pipe", "tensor"))
    return (moe_out, grad_tokens, grad_gates)


def solution(mesh):
    return jax.shard_map(
        per_device,
        mesh=mesh,
        in_specs=(
            P("expert", ("pipe", "tensor")),
            P("expert", None),
            P("expert", None),
            P("expert", None, ("pipe", "tensor")),
            P("expert", None, ("pipe", "tensor")),
            P("expert", ("pipe", "tensor"), None),
            P("expert", ("pipe", "tensor")),
        ),
        out_specs=(
            P("expert", ("pipe", "tensor")),
            P("expert", ("pipe", "tensor")),
            P("expert", None),
        ),
        check_vma=False,
    )
```

profile of v0, /device:TPU:32, one launch (start us, length us, event | category | flops | bytes accessed | tf_op | source)
XLA Modules:
  0.0 457.4 jit_solution(14242704866884179317)
XLA Ops:
  7.2 0.9 copy.35
  9.4 0.8 convert_reduce_fusion
  10.1 0.9 convolution_convert_fusion.1
  11.1 0.9 convolution_convert_fusion.2
  12.1 41.8 %all_to_all.10 = bf16[32,5,768]{2,1,0:T(8,128)(2,1)S(1)} all-to-all(bf16[32,5,768]{2,1,0:T(8,128)(2,1)S(1)} %bitcast.32), channel_id=1, replica_groups=mesh['pipe'=4,'expert'=32,'tensor'=4] {'expert'}, dimensions={0} | all-to-all | bytes 491520 | tf_op jit(solution)/shard_map/all_to_all | solution.py:33
  54.0 0.7 fusion.21
  55.6 54.5 %all-gather.3.cloned.1.call-done = bf16[160,6144]{1,0:T(8,128)(2,1)} async-done(((bf16[160,384]{1,0:T(8,128)(2,1)}), bf16[160,6144]{1,0:T(8,128)(2,1)}) %all-gather.3.cloned.1.call-update) | async-done | bytes 1966096 | tf_op jit(solution)/shard_map/all_gather | solution.py:37
  110.0 2.3 fusion.9
  112.4 2.2 fusion.5
  114.6 60.3 %all-gather.5.cloned.1.call-done = bf16[160,6144]{1,0:T(8,128)(2,1)} async-done(((bf16[160,384]{1,0:T(8,128)(2,1)}), bf16[160,6144]{1,0:T(8,128)(2,1)}) %all-gather.5.cloned.1.call-update) | async-done | bytes 1966096 | tf_op jit(solution)/shard_map/all_gather | solution.py:38
  174.9 2.2 fusion.1
  178.5 1.6 fusion
  180.1 2.8 copy.40
  182.9 2.2 convolution_convert_fusion
  185.1 2.8 copy.38
  187.9 85.6 %reduce-scatter.9.cloned.1.call-done = bf16[384,160]{1,0:T(8,128)(2,1)} async-done(((bf16[6144,160]{1,0:T(8,128)(2,1)}), bf16[384,160]{1,0:T(8,128)(2,1)}) %reduce-scatter.9.cloned.1.call-update) | async-done | bytes 122896
  273.6 1.1 copy.41
  274.6 93.5 %reduce-scatter.7.cloned.1.call-done = bf16[384,160]{1,0:T(8,128)(2,1)} async-done(((bf16[6144,160]{1,0:T(8,128)(2,1)}), bf16[384,160]{1,0:T(8,128)(2,1)}) %reduce-scatter.7.cloned.1.call-update) | async-done | bytes 122896
  368.1 1.1 copy.39
  369.2 0.8 reshape.67
  370.1 12.8 %all-to-all-start.1 = ((bf16[32,5,768]{2,1,0:T(8,128)(2,1)}), bf16[32,5,768]{2,1,0:T(8,128)(2,1)S(1)}, u32[]{:S(2)}, u32[]{:S(2)}) async-start(bf16[32,5,768]{2,1,0:T(8,128)(2,1)} %reshape.67), calls=%async_computation.1 | async-start | bytes 786432 | tf_op jit(solution)/shard_map/all_to_all | solution.py:68
  383.0 26.5 %all-to-all-done.1 = bf16[32,5,768]{2,1,0:T(8,128)(2,1)S(1)} async-done(((bf16[32,5,768]{2,1,0:T(8,128)(2,1)}), bf16[32,5,768]{2,1,0:T(8,128)(2,1)S(1)}, u32[]{:S(2)}, u32[]{:S(2)}) %all-to-all-start.1) | async-done | bytes 245792 | tf_op jit(solution)/shard_map/all_to_all | solution.py:68
  410.2 38.6 %psum.7 = f32[16,2]{1,0:T(8,128)S(1)} all-reduce(f32[16,2]{1,0:T(8,128)S(1)} %reduce_sum.72), channel_id=1, replica_groups=mesh['pipe'=4,'expert'=32,'tensor'=4] {'pipe','tensor'}, use_global_device_ids=true, to_apply=%region_10.11 | all-reduce | flops 32 | bytes 256 | tf_op jit(solution)/shard_map/psum | solution.py:81
  449.5 0.7 multiply_reduce_fusion.1
  (50 shorter events, 5.8 us)
Async XLA Ops:
  7.2 102.9 %copy-start = (bf16[1,6144,128]{2,1,0:T(8,128)(2,1)S(1)}, bf16[1,6144,128]{2,1,0:T(8,128)(2,1)}, u32[]{:S(2)}) copy-start(bf16[1,6144,128]{2,1,0:T(8,128)(2,1)} %param.10) | copy-start | bytes 4718596
  7.2 102.8 %all-gather.3.cloned.1.call-start = ((), (), s32[]{:S(2)}) async-start(), calls=%async_computation.4 | async-start | bytes 2088960 | tf_op jit(solution)/shard_map/all_gather | solution.py:37
  54.8 120.1 %all-gather.5.cloned.1.call-start = ((), (), s32[]{:S(2)}) async-start(), calls=%async_computation.5 | async-start | bytes 2088960 | tf_op jit(solution)/shard_map/all_gather | solution.py:38
  55.5 218.1 %reduce-scatter.9.cloned.1.call-start = ((), (), s32[]{:S(2)}) async-start(), calls=%async_computation.7 | async-start | bytes 3342336
  110.0 2.4 copy-start.1
  112.4 64.7 %copy-start.4 = (f32[160,128]{1,0:T(8,128)}, f32[160,128]{1,0:T(8,128)S(1)}, u32[]{:S(2)}) copy-start(f32[160,128]{1,0:T(8,128)S(1)} %fusion.9) | copy-start | bytes 245764
  112.4 62.5 %copy-start.2 = (bf16[1,128,6144]{2,1,0:T(8,128)(2,1)S(1)}, bf16[1,128,6144]{2,1,0:T(8,128)(2,1)}, u32[]{:S(2)}) copy-start(bf16[1,128,6144]{2,1,0:T(8,128)(2,1)} %param.12) | copy-start | bytes 4718596
  114.6 62.5 %copy-start.5 = (f32[160,128]{1,0:T(8,128)}, f32[160,128]{1,0:T(8,128)S(1)}, u32[]{:S(2)}) copy-start(f32[160,128]{1,0:T(8,128)S(1)} %fusion.5) | copy-start | bytes 245764
  177.1 1.4 copy-start.3
  182.9 185.2 %reduce-scatter.7.cloned.1.call-start = ((), (), s32[]{:S(2)}) async-start(), calls=%async_computation.6 | async-start | bytes 3342336
  187.9 195.0 %copy-start.7 = (f32[16,2]{0,1:T(2,128)S(1)}, f32[16,2]{0,1:T(2,128)}, u32[]{:S(2)}) copy-start(f32[16,2]{0,1:T(2,128)} %param.9) | copy-start | bytes 388
  187.9 195.1 %copy-start.6 = (bf16[16,384]{1,0:T(8,128)(2,1)S(1)}, bf16[16,384]{1,0:T(8,128)(2,1)}, u32[]{:S(2)}) copy-start(bf16[16,384]{1,0:T(8,128)(2,1)} %param.13) | copy-start | bytes 36868
  370.1 39.5 %all-to-all-start.1 = ((bf16[32,5,768]{2,1,0:T(8,128)(2,1)}), bf16[32,5,768]{2,1,0:T(8,128)(2,1)S(1)}, u32[]{:S(2)}, u32[]{:S(2)}) async-start(bf16[32,5,768]{2,1,0:T(8,128)(2,1)} %reshape.67), calls=%async_computation.1 | async-start | bytes 786432 | tf_op jit(solution)/shard_map/all_to_all | solution.py:68
Sparse Core Ops, SparseCore 0:
  54.9 55.0 all-gather.2
  113.0 61.8 all-gather.4
  183.0 90.5 reduce-scatter.8
  277.6 90.4 reduce-scatter.6
where the time goes:
time: 458 us; the launch traced here: 457 us
  waiting for transfers between devices  321 us (70%)
  blocking collectives  80.5 us (18%)
  between operations  14 us (3%)
  matrix products  13.2 us (3%)
  starting transfers between devices  13 us (3%)
  local copies, waits for them, and re-layouts  12.2 us (3%)
    unnamed x6, waiting for transfers between devices  180 us
    all_gather x1, waiting for transfers between devices, per_device(): rows_dy = lax.all_gather(part_dy, ('pipe', 'tensor'), axis=1, tiled=True)  60.3 us
    all_gather x1, waiting for transfers between devices, per_device(): rows_x = lax.all_gather(part_x, ('pipe', 'tensor'), axis=1, tiled=True)  54.5 us
    all_to_all x1, blocking collectives, per_device(): lax.all_to_all(send, 'expert', split_axis=0, concat_axis=0, tiled=True)  41.8 us
    psum x1, blocking collectives, per_device(): grad_gates = lax.psum(partial_dots, ('pipe', 'tensor'))  38.6 us
    all_to_all x1, waiting for transfers between devices, per_device(): lax.all_to_all(back_send, 'expert', split_axis=0, concat_axis=0, tiled=True)  26.5 us
    all_to_all x1, starting transfers between devices, per_device(): lax.all_to_all(back_send, 'expert', split_axis=0, concat_axis=0, tiled=True)  12.8 us
    unnamed x23, local copies, waits for them, and re-layouts  9.97 us
  transfers between devices with their start and end apart: 5, of which 5 were waited for; matrix products, arithmetic and copies ran while one was open for 2% of the time, Pallas kernels for 0%

commit v1 on v0

--- a/solution.py
+++ b/solution.py
@@ -34,8 +34,13 @@
     recv = recv.reshape(devices_all * capacity, 2 * feat)
     part_x = recv[:, :feat]
     part_dy = recv[:, feat:]
-    rows_x = lax.all_gather(part_x, ("pipe", "tensor"), axis=1, tiled=True)
-    rows_dy = lax.all_gather(part_dy, ("pipe", "tensor"), axis=1, tiled=True)
+    rows_x, rows_dy = jnp.split(
+        lax.all_gather(
+            jnp.concatenate([part_x, part_dy], axis=0), ("pipe", "tensor"), axis=1, tiled=True
+        ),
+        [part_x.shape[0]],
+        axis=0,
+    )
     gate_proj = w_gate[0]
     up_proj = w_up[0]
     down_proj = w_down[0]

time: 458 us -> 405 us (0.88)
  waiting for transfers between devices: 321 us -> 270 us
    all_gather x2 -> x1, waiting for transfers between devices: 115 us -> 64.5 us  [per_device(): lax.all_gather(jnp.concatenate([part_x, part_dy], axis=0), ('pipe', 'tens...]
    unnamed x6 -> x5, waiting for transfers between devices: 180 us -> 179 us
  transfers between devices with their start and end apart: 5 -> 4, of which waited for: 5 -> 4; matrix products, arithmetic and copies ran while one was open for 2% -> 2% of each run, Pallas kernels for 0% -> 0%
where the time goes in v1:
time: 405 us; the launch traced here: 404 us
  waiting for transfers between devices  270 us (67%)
  blocking collectives  80.5 us (20%)
  between operations  14 us (3%)
  starting transfers between devices  12.9 us (3%)
  local copies, waits for them, and re-layouts  11.4 us (3%)
  matrix products  11 us (3%)
  other arithmetic  4.13 us (1%)
    unnamed x5, waiting for transfers between devices  179 us
    all_gather x1, waiting for transfers between devices, per_device(): lax.all_gather(jnp.concatenate([part_x, part_dy], axis=0), ('pipe', 'tens...  64.5 us
    all_to_all x1, blocking collectives, per_device(): lax.all_to_all(send, 'expert', split_axis=0, concat_axis=0, tiled=True)  41.8 us
    psum x1, blocking collectives, per_device(): grad_gates = lax.psum(partial_dots, ('pipe', 'tensor'))  38.7 us
    all_to_all x1, waiting for transfers between devices, per_device(): lax.all_to_all(back_send, 'expert', split_axis=0, concat_axis=0, tiled=True)  26.5 us
    all_to_all x1, starting transfers between devices, per_device(): lax.all_to_all(back_send, 'expert', split_axis=0, concat_axis=0, tiled=True)  12.8 us
    unnamed x23, local copies, waits for them, and re-layouts  9.88 us
  transfers between devices with their start and end apart: 4, of which 4 were waited for; matrix products, arithmetic and copies ran while one was open for 2% of the time, Pallas kernels for 0%

profile of v1, /device:TPU:32, one launch (start us, length us, event | category | flops | bytes accessed | tf_op | source)
XLA Modules:
  0.0 404.2 jit_solution(18309476877020868811)
XLA Ops:
  7.2 0.9 copy.35
  8.7 0.7 multiply_add_fusion
  9.4 0.8 convert_reduce_fusion
  10.1 0.9 convolution_convert_fusion.1
  11.1 0.9 convolution_convert_fusion.2
  12.1 41.8 %all_to_all.10 = bf16[32,5,768]{2,1,0:T(8,128)(2,1)S(1)} all-to-all(bf16[32,5,768]{2,1,0:T(8,128)(2,1)S(1)} %bitcast.29), channel_id=1, replica_groups=mesh['pipe'=4,'expert'=32,'tensor'=4] {'expert'}, dimensions={0} | all-to-all | bytes 491520 | tf_op jit(solution)/shard_map/all_to_all | solution.py:33
  54.1 0.7 pad_maximum_fusion
  54.9 64.5 %all-gather.2.cloned.1.call-done = bf16[320,6144]{1,0:T(8,128)(2,1)} async-done(((bf16[320,384]{1,0:T(8,128)(2,1)}), bf16[320,6144]{1,0:T(8,128)(2,1)}) %all-gather.2.cloned.1.call-update) | async-done | bytes 3932176 | tf_op jit(solution)/shard_map/all_gather | solution.py:38
  119.3 2.4 fusion.5
  121.7 2.4 fusion.1
  124.1 0.7 fusion.3
  126.1 0.7 fusion
  126.8 2.8 copy.40
  129.7 2.2 convolution_convert_fusion
  131.8 2.8 copy.38
  134.7 85.7 %reduce-scatter.9.cloned.1.call-done = bf16[384,160]{1,0:T(8,128)(2,1)} async-done(((bf16[6144,160]{1,0:T(8,128)(2,1)}), bf16[384,160]{1,0:T(8,128)(2,1)}) %reduce-scatter.9.cloned.1.call-update) | async-done | bytes 122896
  220.3 1.1 copy.41
  221.4 93.6 %reduce-scatter.7.cloned.1.call-done = bf16[384,160]{1,0:T(8,128)(2,1)} async-done(((bf16[6144,160]{1,0:T(8,128)(2,1)}), bf16[384,160]{1,0:T(8,128)(2,1)}) %reduce-scatter.7.cloned.1.call-update) | async-done | bytes 122896
  315.0 1.1 copy.39
  316.1 0.8 reshape.67
  316.9 12.8 %all-to-all-start.1 = ((bf16[32,5,768]{2,1,0:T(8,128)(2,1)}), bf16[32,5,768]{2,1,0:T(8,128)(2,1)S(1)}, u32[]{:S(2)}, u32[]{:S(2)}) async-start(bf16[32,5,768]{2,1,0:T(8,128)(2,1)} %reshape.67), calls=%async_computation.1 | async-start | bytes 786432 | tf_op jit(solution)/shard_map/all_to_all | solution.py:73
  329.9 26.5 %all-to-all-done.1 = bf16[32,5,768]{2,1,0:T(8,128)(2,1)S(1)} async-done(((bf16[32,5,768]{2,1,0:T(8,128)(2,1)}), bf16[32,5,768]{2,1,0:T(8,128)(2,1)S(1)}, u32[]{:S(2)}, u32[]{:S(2)}) %all-to-all-start.1) | async-done | bytes 245792 | tf_op jit(solution)/shard_map/all_to_all | solution.py:73
  357.0 38.7 %psum.7 = f32[16,2]{1,0:T(8,128)S(1)} all-reduce(f32[16,2]{1,0:T(8,128)S(1)} %reduce_sum.72), channel_id=1, replica_groups=mesh['pipe'=4,'expert'=32,'tensor'=4] {'pipe','tensor'}, use_global_device_ids=true, to_apply=%region_10.11 | all-reduce | flops 32 | bytes 256 | tf_op jit(solution)/shard_map/psum | solution.py:86
  396.3 0.7 multiply_reduce_fusion.1
  (48 shorter events, 4.3 us)
Async XLA Ops:
  7.2 112.2 %copy-start = (bf16[1,6144,128]{2,1,0:T(8,128)(2,1)S(1)}, bf16[1,6144,128]{2,1,0:T(8,128)(2,1)}, u32[]{:S(2)}) copy-start(bf16[1,6144,128]{2,1,0:T(8,128)(2,1)} %param.10) | copy-start | bytes 4718596
  7.2 112.1 %all-gather.2.cloned.1.call-start = ((), (), s32[]{:S(2)}) async-start(), calls=%async_computation.4 | async-start | bytes 4177920 | tf_op jit(solution)/shard_map/all_gather | solution.py:38
  54.8 66.9 %copy-start.1 = (bf16[1,128,6144]{2,1,0:T(8,128)(2,1)S(1)}, bf16[1,128,6144]{2,1,0:T(8,128)(2,1)}, u32[]{:S(2)}) copy-start(bf16[1,128,6144]{2,1,0:T(8,128)(2,1)} %param.12) | copy-start | bytes 4718596
  54.8 165.5 %reduce-scatter.9.cloned.1.call-start = ((), (), s32[]{:S(2)}) async-start(), calls=%async_computation.6 | async-start | bytes 3342336
  119.3 4.8 %copy-start.7 = (bf16[320,6144]{1,0:T(8,128)(2,1)S(1)}, bf16[320,6144]{1,0:T(8,128)(2,1)}, u32[]{:S(2)}) copy-start(bf16[320,6144]{1,0:T(8,128)(2,1)} %all-gather.2.cloned.1.call-done) | copy-start | bytes 11796484
  121.7 4.4 %copy-start.3 = (f32[160,128]{1,0:T(8,128)}, f32[160,128]{1,0:T(8,128)S(1)}, u32[]{:S(2)}) copy-start(f32[160,128]{1,0:T(8,128)S(1)} %fusion.5) | copy-start | bytes 245764
  121.7 2.4 copy-start.2
  124.8 0.6 copy-start.4
  129.6 185.4 %reduce-scatter.7.cloned.1.call-start = ((), (), s32[]{:S(2)}) async-start(), calls=%async_computation.5 | async-start | bytes 3342336
  134.6 195.1 %copy-start.6 = (f32[16,2]{0,1:T(2,128)S(1)}, f32[16,2]{0,1:T(2,128)}, u32[]{:S(2)}) copy-start(f32[16,2]{0,1:T(2,128)} %param.9) | copy-start | bytes 388
  134.6 195.2 %copy-start.5 = (bf16[16,384]{1,0:T(8,128)(2,1)S(1)}, bf16[16,384]{1,0:T(8,128)(2,1)}, u32[]{:S(2)}) copy-start(bf16[16,384]{1,0:T(8,128)(2,1)} %param.13) | copy-start | bytes 36868
  316.9 39.5 %all-to-all-start.1 = ((bf16[32,5,768]{2,1,0:T(8,128)(2,1)}), bf16[32,5,768]{2,1,0:T(8,128)(2,1)S(1)}, u32[]{:S(2)}, u32[]{:S(2)}) async-start(bf16[32,5,768]{2,1,0:T(8,128)(2,1)} %reshape.67), calls=%async_computation.1 | async-start | bytes 786432 | tf_op jit(solution)/shard_map/all_to_all | solution.py:73
Sparse Core Ops, SparseCore 0:
  54.9 64.3 all-gather.1
  129.7 90.5 reduce-scatter.8
  224.5 90.4 reduce-scatter.6
